TPU v7x, 32 devices: a whole 2x2x4 slice. The times are simulated.
32 devices in a mesh: seq: 16 (over z, y, core), dp: 2 (over x).
Axes of the slice: x: 2, y: 2, z: 4, core: 2. Of those that a mesh axis runs over, the one named last changes fastest.
Arguments:
- query_rows: bfloat16 [2, 4096, 768], P('dp', 'seq'), may hold values from -40 to 40
- key_rows: bfloat16 [2, 4096, 768], P('dp', 'seq'), may hold values from -40 to 40
- value_rows: bfloat16 [2, 4096, 768], P('dp', 'seq'), may hold values from -6 to 6
- out_grad: bfloat16 [2, 4096, 1536], P('dp', 'seq'), may hold values from -6 to 6
- lengths: int32 [2, 8], P('dp'), may hold values from 1 to 1024, 4096 in all within a row
- out_weight: bfloat16 [768, 1536], P('seq', 'dp'), may hold values from -0.21875 to 0.21875
Outputs:
- mixed_out: bfloat16 [2, 4096, 1536], P('dp', 'seq')
- query_grad: bfloat16 [2, 4096, 768], P('dp', 'seq')
- key_grad: bfloat16 [2, 4096, 768], P('dp', 'seq')
- value_grad: bfloat16 [2, 4096, 768], P('dp', 'seq')
- weight_grad: float32 [768, 1536], P('seq', 'dp')
Inputs may be any that keep to these rules, and one draw needn't show every extreme that they name: Each row holds the lengths of the 8 utterances of one group in packing order; they sum to 4096 and the longest is exactly 1024.
All inputs are finite; a program needn't handle non-finite values.
Results may differ from a plain program's by a relative error of at most 0.022.
Values may be sent and summed in bfloat16 or wider, within the bound.
No kernel may reach another device: no remote copies, remote signals or barrier semaphores. Data moves between devices by JAX's collectives and lax.ppermute only.
A program may use at most 64 MiB of HBM per device.

v0:
```python
import jax
import jax.numpy as jnp
from jax import lax
from jax.sharding import PartitionSpec as P

HEADS = 12
HEAD_DIM = 64
STRETCH = 128
MOST = 1024
MASKED_SCORE = -1e30


def shift_up(block, axis, distance):
    devices = range(lax.axis_size(axis))
    route = [(i - distance, i) for i in devices if i - distance in devices]
    return lax.ppermute(block, axis, route)


def frame_labels(utt_lengths, first_frame, frame_count, total_frames):
    positions = first_frame + jnp.arange(frame_count, dtype=jnp.int32)
    utt_ends = jnp.cumsum(utt_lengths)
    utt_index = jnp.sum((positions[:, None] >= utt_ends[None, :]).astype(jnp.int32), axis=1)
    outside = (positions < 0) | (positions >= total_frames)
    return (jnp.where(outside, -1, utt_index), positions // STRETCH)


def local(query_rows, key_rows, value_rows, out_grad, lengths, out_weight):
    seq_count = lax.axis_size("seq")
    device = lax.axis_index("seq")
    tok_rows = query_rows.shape[1]
    feature_width = query_rows.shape[2]
    total_frames = seq_count * tok_rows
    reach = min(-(-MOST // tok_rows), seq_count - 1)
    window = (reach + 1) * tok_rows
    score_scale = HEAD_DIM ** (-0.5)
    utt_lengths = lengths[0]
    weight_cols = lax.all_gather(out_weight, "dp", axis=1, tiled=True)
    weight_full = lax.all_gather(weight_cols, "seq", axis=0, tiled=True)
    query_heads = query_rows[0].reshape(tok_rows, HEADS, HEAD_DIM)
    key_value = jnp.concatenate([key_rows[0], value_rows[0]], axis=1)
    held = [key_value]
    for _ in range(reach):
        held.append(shift_up(held[-1], "seq", 1))
    kv_window = jnp.concatenate(held[::-1], axis=0)
    key_window = kv_window[:, :feature_width].reshape(window, HEADS, HEAD_DIM)
    value_window = kv_window[:, feature_width:].reshape(window, HEADS, HEAD_DIM)
    query_utt, query_stretch = frame_labels(utt_lengths, device * tok_rows, tok_rows, total_frames)
    key_utt, key_stretch = frame_labels(
        utt_lengths, (device - reach) * tok_rows, window, total_frames
    )
    visible = (query_utt[:, None] == key_utt[None, :]) & (
        key_stretch[None, :] <= query_stretch[:, None]
    )
    scores = (
        jnp.einsum("qhe,khe->hqk", query_heads, key_window, preferred_element_type=jnp.float32)
        * score_scale
    )
    masked = jnp.where(visible[None], scores, MASKED_SCORE)
    top_score = jnp.max(masked, axis=2)
    expo_full = jnp.where(visible[None], jnp.exp(masked - top_score[:, :, None]), 0.0)
    row_sum = jnp.sum(expo_full, axis=2)
    weighted = jnp.einsum(
        "hqk,khe->qhe",
        expo_full.astype(jnp.bfloat16),
        value_window,
        preferred_element_type=jnp.float32,
    )
    attended = (
        (weighted / jnp.transpose(row_sum)[:, :, None])
        .reshape(tok_rows, feature_width)
        .astype(jnp.bfloat16)
    )
    log_sum = top_score + jnp.log(row_sum)
    mixed_out = jnp.dot(attended, weight_full, preferred_element_type=jnp.float32).astype(
        jnp.bfloat16
    )
    upstream = out_grad[0]
    att_grad = lax.dot_general(
        upstream, weight_full, (((1,), (1,)), ((), ())), preferred_element_type=jnp.float32
    ).astype(jnp.bfloat16)
    partial_weight = lax.dot_general(
        attended, upstream, (((0,), (0,)), ((), ())), preferred_element_type=jnp.float32
    )
    col_share = lax.psum_scatter(partial_weight, "dp", scatter_dimension=1, tiled=True)
    weight_grad = lax.psum_scatter(col_share, "seq", scatter_dimension=0, tiled=True)
    grad_heads = att_grad.reshape(tok_rows, HEADS, HEAD_DIM)
    delta_rows = jnp.sum(
        grad_heads.astype(jnp.float32)
        * attended.reshape(tok_rows, HEADS, HEAD_DIM).astype(jnp.float32),
        axis=2,
    )
    query_acc = jnp.zeros((tok_rows, HEADS, HEAD_DIM), jnp.float32)
    carried = None
    for back in range(reach, -1, -1):
        rows = slice((reach - back) * tok_rows, (reach - back + 1) * tok_rows)
        key_block = key_window[rows]
        value_block = value_window[rows]
        block_visible = visible[:, rows]
        block_scores = (
            jnp.einsum("qhe,khe->hqk", query_heads, key_block, preferred_element_type=jnp.float32)
            * score_scale
        )
        prob_full = jnp.where(block_visible[None], jnp.exp(block_scores - log_sum[:, :, None]), 0.0)
        prob_back = prob_full.astype(jnp.bfloat16)
        prob_grad = jnp.einsum(
            "qhe,khe->hqk", grad_heads, value_block, preferred_element_type=jnp.float32
        )
        score_grad = (prob_full * (prob_grad - jnp.transpose(delta_rows)[:, :, None])).astype(
            jnp.bfloat16
        )
        query_acc = query_acc + jnp.einsum(
            "hqk,khe->qhe", score_grad, key_block, preferred_element_type=jnp.float32
        )
        key_part = (
            jnp.einsum("hqk,qhe->khe", score_grad, query_heads, preferred_element_type=jnp.float32)
            * score_scale
        )
        value_part = jnp.einsum(
            "hqk,qhe->khe", prob_back, grad_heads, preferred_element_type=jnp.float32
        )
        part = jnp.concatenate(
            [
                key_part.reshape(tok_rows, feature_width),
                value_part.reshape(tok_rows, feature_width),
            ],
            axis=1,
        )
        if carried is None:
            carried = part
        else:
            carried = shift_up(carried, "seq", -1) + part
    query_grad = (query_acc * score_scale).reshape(tok_rows, feature_width).astype(jnp.bfloat16)
    key_grad = carried[:, :feature_width].astype(jnp.bfloat16)
    value_grad = carried[:, feature_width:].astype(jnp.bfloat16)
    return (mixed_out[None], query_grad[None], key_grad[None], value_grad[None], weight_grad)


def solution(mesh):
    return jax.shard_map(
        local,
        mesh=mesh,
        in_specs=(
            P("dp", "seq", None),
            P("dp", "seq", None),
            P("dp", "seq", None),
            P("dp", "seq", None),
            P("dp", None),
            P("seq", "dp"),
        ),
        out_specs=(
            P("dp", "seq", None),
            P("dp", "seq", None),
            P("dp", "seq", None),
            P("dp", "seq", None),
            P("seq", "dp"),
        ),
        check_vma=False,
    )
```

profile of v0, /device:TPU:0, one launch (start us, length us, event | category | flops | bytes accessed | tf_op | source)
XLA Modules:
  0.0 278.8 jit_solution(4228232559934887295)
XLA Ops:
  12.7 11.6 %collective-permute-start.1 = (bf16[256,1536]{1,0:T(8,128)(2,1)S(1)}, bf16[256,1536]{1,0:T(8,128)(2,1)S(1)}, u32[]{:S(2)}, u32[]{:S(2)}) collective-permute-start(bf16[256,1536]{1,0:T(8,128)(2,1)S(1)} %collective-permute-done), channel_id=1, source_target_pairs={{0,2},{2,4},{4,6},{6,8},{8,10},{10,12},{12,14},{14,16},{16,18},{18... | collective-permute-start | bytes 2359304 | tf_op jit(solution)/shard_map/ppermute | solution.py:16
  26.2 11.4 %collective-permute-start.2 = (bf16[256,1536]{1,0:T(8,128)(2,1)S(1)}, bf16[256,1536]{1,0:T(8,128)(2,1)S(1)}, u32[]{:S(2)}, u32[]{:S(2)}) collective-permute-start(bf16[256,1536]{1,0:T(8,128)(2,1)S(1)} %collective-permute-done.1), channel_id=1, source_target_pairs={{0,2},{2,4},{4,6},{6,8},{8,10},{10,12},{12,14},{14,16},{16,18},{18... | collective-permute-start | bytes 2359304 | tf_op jit(solution)/shard_map/ppermute | solution.py:16
  37.6 6.3 %all_gather.6 = bf16[48,1536]{1,0:T(8,128)(2,1)} all-gather(bf16[48,768]{1,0:T(8,128)(2,1)} %param.11), channel_id=1, replica_groups=mesh['seq'=16,'dp'=2] {'dp'}, dimensions={1}, use_global_device_ids=true | all-gather | bytes 221184 | tf_op jit(solution)/shard_map/all_gather | solution.py:37
  45.0 6.8 %collective-permute-start.3 = (bf16[256,1536]{1,0:T(8,128)(2,1)S(1)}, bf16[256,1536]{1,0:T(8,128)(2,1)}, u32[]{:S(2)}, u32[]{:S(2)}) collective-permute-start(bf16[256,1536]{1,0:T(8,128)(2,1)S(1)} %collective-permute-done.2), channel_id=1, source_target_pairs={{0,2},{2,4},{4,6},{6,8},{8,10},{10,12},{12,14},{14,16},{16,18},{18... | collective-permute-start | bytes 2359304 | tf_op jit(solution)/shard_map/ppermute | solution.py:16
  57.1 4.0 %copy.117 = bf16[1280,768]{0,1:T(8,128)(2,1)} copy(bf16[1280,768]{1,0:T(8,128)(2,1)} %get-tuple-element.20) | data formatting | bytes 3932160 | tf_op jit(solution)/shard_map/slice | solution.py:45
  63.4 9.6 %fusion = (f32[12,256]{1,0:T(8,128)S(1)}, f32[12,1280,256]{2,1,0:T(8,128)}) fusion(pred[256,1280]{0,1:T(8,128)(4,1)S(1)} %compare_and_fusion, bf16[1280,12,64]{0,2,1:T(8,128)(2,1)} %bitcast.189, bf16[256,12,64]{0,2,1:T(8,128)(2,1)S(1)} %bitcast.178), kind=kOutput, calls=%fused_computation.2 | convolution fusion | flops 515109888 | bytes 18427904 | tf_op jit(solution)/shard_map/qhe,khe->hqk/dot_general | solution.py:55
  73.0 9.2 %fusion.1 = f32[12,256]{1,0:T(8,128)S(1)} fusion(f32[12,1280,256]{2,1,0:T(8,128)} %get-tuple-element.38, f32[12,256]{1,0:T(8,128)S(1)} %get-tuple-element.37, pred[256,1280]{0,1:T(8,128)(4,1)S(1)} %compare_and_fusion), kind=kLoop, calls=%fused_computation.3 | loop fusion | flops 19657728 | bytes 16080896 | tf_op jit(solution)/shard_map/reduce_sum | solution.py:61
  82.2 7.5 %all-gather.2.cloned.1.call-done = bf16[768,1536]{1,0:T(8,128)(2,1)} async-done(((bf16[48,1536]{1,0:T(8,128)(2,1)}), bf16[768,1536]{1,0:T(8,128)(2,1)}) %all-gather.2.cloned.1.call-update) | async-done | bytes 2359312 | tf_op jit(solution)/shard_map/all_gather | solution.py:38
  89.7 2.5 convolution_convert_fusion.1
  92.3 10.0 %multiply_reduce_fusion = (f32[256,12]{0,1:T(8,128)S(1)}, bf16[256,12,64]{0,2,1:T(8,128)(2,1)S(1)}) fusion(bf16[256,12,64]{0,2,1:T(8,128)(2,1)S(1)} %bitcast.194, f32[256,12]{0,1:T(8,128)S(1)} %bitcast.234, bf16[1280,12,64]{0,2,1:T(8,128)(2,1)} %bitcast.223, f32[12,1280,256]{2,1,0:T(8,128)} %get-tuple-element.38, f32[12,256]{1,0:T(8,128)S(1)} %get-tuple-element.37, ...), kind=kOutput, calls=%fused_computation.75 | convolution fusion | flops 524153856 | bytes 18845696 | tf_op jit(solution)/shard_map/hqk,khe->qhe/dot_general | solution.py:62
  103.0 2.9 %fusion.54 = f32[768,1536]{1,0:T(8,128)} fusion(bf16[256,768]{0,1:T(8,128)(2,1)S(1)} %bitcast.221, bf16[1,256,1536]{2,1,0:T(8,128)(2,1)S(1)} %copy-done), kind=kOutput, calls=%fused_computation.72 | convolution fusion | flops 603979776 | bytes 5898240 | tf_op jit(solution)/shard_map/dot_general | solution.py:81
  121.8 3.5 %fusion.17 = f32[12,64,256]{2,1,0:T(8,128)} fusion(bf16[256,12,64]{0,2,1:T(8,128)(2,1)S(1)} %bitcast.196, f32[12,256,256]{2,1,0:T(8,128)} %copy-done.27, f32[12,256]{1,0:T(8,128)S(1)} %log_add_fusion, pred[256,256]{0,1:T(8,128)(4,1)} %copy-done.37), kind=kOutput, calls=%fused_computation.27 | convolution fusion | flops 103809024 | bytes 4403200 | tf_op jit(solution)/shard_map/hqk,qhe->khe/dot_general | solution.py:118
  139.5 3.5 %fusion.15 = f32[12,64,256]{2,1,0:T(8,128)} fusion(bf16[256,12,64]{0,2,1:T(8,128)(2,1)S(1)} %bitcast.198, f32[12,256,256]{2,1,0:T(8,128)} %copy-done.28, f32[12,256]{1,0:T(8,128)S(1)} %log_add_fusion, pred[256,256]{0,1:T(8,128)(4,1)} %get-tuple-element.36), kind=kOutput, calls=%fused_computation.26 | convolution fusion | flops 103809024 | bytes 4403200 | tf_op jit(solution)/shard_map/hqk,qhe->khe/dot_general | solution.py:118
  145.4 3.3 %maximum_add_fusion = f32[256,1536]{1,0:T(8,128)} fusion(f32[256,1536]{1,0:T(8,128)} %collective-permute-done.4, f32[256,768]{1,0:T(8,128)} %copy.149, f32[256,768]{1,0:T(8,128)} %copy.148), kind=kLoop, calls=%fused_computation.30 | loop fusion | flops 786432 | bytes 4718592 | tf_op jit(solution)/shard_map/add | solution.py:131
  152.7 3.6 %copy.138 = f32[12,256,256]{1,2,0:T(8,128)} copy(f32[12,256,256]{2,1,0:T(8,128)} %subtract_exponential_fusion) | data formatting | bytes 6291456 | tf_op jit(solution)/shard_map/exp | solution.py:103
  156.3 3.0 %multiply_convert_fusion.2 = bf16[12,256,256]{1,2,0:T(8,128)(2,1)S(1)} fusion(f32[12,256,256]{2,1,0:T(8,128)} %fusion.84, bf16[256,12,64]{0,2,1:T(8,128)(2,1)S(1)} %bitcast.199, bf16[256,12,64]{0,2,1:T(8,128)(2,1)} %bitcast.231, f32[12,256]{1,0:T(8,128)} %bitcast.237, f32[12,256]{1,0:T(8,128)S(1)} %log_add_fusion, pred[256,256]{0,1:T(8,128)(4,1)} %get-tuple-element.35), kind=kOutput, calls=%fused_computation.14 | convolution fusion | flops 105381888 | bytes 5595136 | tf_op jit(solution)/shard_map/qhe,khe->hqk/dot_general | solution.py:105
  164.3 3.5 %fusion.13 = f32[12,64,256]{2,1,0:T(8,128)} fusion(bf16[256,12,64]{0,2,1:T(8,128)(2,1)S(1)} %bitcast.200, f32[12,256,256]{2,1,0:T(8,128)} %fusion.84, f32[12,256]{1,0:T(8,128)S(1)} %log_add_fusion, pred[256,256]{0,1:T(8,128)(4,1)} %get-tuple-element.35), kind=kOutput, calls=%fused_computation.25 | convolution fusion | flops 103809024 | bytes 4403200 | tf_op jit(solution)/shard_map/hqk,qhe->khe/dot_general | solution.py:118
  170.1 3.5 %fusion.19 = f32[12,64,256]{2,1,0:T(8,128)} fusion(bf16[256,12,64]{0,2,1:T(8,128)(2,1)S(1)} %bitcast.201, f32[12,256,256]{1,2,0:T(8,128)} %copy.138, pred[256,256]{0,1:T(8,128)(4,1)} %get-tuple-element.33), kind=kOutput, calls=%fused_computation.28 | convolution fusion | flops 101449728 | bytes 4390912 | tf_op jit(solution)/shard_map/hqk,qhe->khe/dot_general | solution.py:118
  173.6 3.0 %maximum_add_fusion.1 = f32[256,1536]{1,0:T(8,128)} fusion(f32[256,1536]{1,0:T(8,128)} %collective-permute-done.5, f32[256,768]{1,0:T(8,128)S(1)} %copy-done.18, f32[256,768]{1,0:T(8,128)S(1)} %copy-done.17), kind=kLoop, calls=%fused_computation.31 | loop fusion | flops 786432 | bytes 4718592 | tf_op jit(solution)/shard_map/add | solution.py:131
  188.2 2.8 multiply_convert_fusion
  192.8 2.8 maximum_add_fusion.2
  208.6 3.5 %fusion.6 = bf16[1,256,1536]{2,1,0:T(8,128)(2,1)} fusion(bf16[256,768]{0,1:T(8,128)(2,1)S(1)} %bitcast.222, bf16[768,1536]{1,0:T(8,128)(2,1)} %all-gather.2.cloned.1.call-done), kind=kOutput, calls=%fused_computation.19 | convolution fusion | flops 604372992 | bytes 3538944 | tf_op jit(solution)/shard_map/dot_general | solution.py:74
  212.1 5.5 %collective-permute-done.7 = f32[256,1536]{1,0:T(8,128)} collective-permute-done((f32[256,1536]{1,0:T(8,128)}, f32[256,1536]{1,0:T(8,128)}, u32[]{:S(2)}, u32[]{:S(2)}) %collective-permute-start.7) | collective-permute-done | bytes 1572896 | tf_op jit(solution)/shard_map/ppermute | solution.py:16
  220.2 52.1 %reduce-scatter.5.cloned.1.call-done = f32[48,768]{1,0:T(8,128)} async-done(((f32[768,768]{1,0:T(8,128)}), f32[48,768]{1,0:T(8,128)}) %reduce-scatter.5.cloned.1.call-update) | async-done | bytes 147472 | tf_op jit(solution)/shard_map/reduce_scatter | solution.py:85
  (168 shorter events, 89.3 us)
Async XLA Ops:
  7.2 82.5 %copy-start = (bf16[1,256,1536]{2,1,0:T(8,128)(2,1)S(1)}, bf16[1,256,1536]{2,1,0:T(8,128)(2,1)}, u32[]{:S(2)}) copy-start(bf16[1,256,1536]{2,1,0:T(8,128)(2,1)} %param.9) | copy-start | bytes 2359300
  7.2 82.5 %all-gather.2.cloned.1.call-start = ((), (), s32[]{:S(2)}) async-start(), calls=%async_computation.2 | async-start | bytes 2506752 | tf_op jit(solution)/shard_map/all_gather | solution.py:38
  8.5 4.3 %collective-permute-start = (bf16[256,1536]{1,0:T(8,128)(2,1)S(1)}, bf16[256,1536]{1,0:T(8,128)(2,1)S(1)}, u32[]{:S(2)}, u32[]{:S(2)}) collective-permute-start(bf16[256,1536]{1,0:T(8,128)(2,1)S(1)} %pad_maximum_fusion.1), channel_id=1, source_target_pairs={{0,2},{2,4},{4,6},{6,8},{8,10},{10,12},{12,14},{14,16},{16,18},{18... | collective-permute-start | bytes 2359304 | tf_op jit(solution)/shard_map/ppermute | solution.py:16
  12.7 13.5 %copy-start.23 = (bf16[256,1536]{1,0:T(8,128)(2,1)}, bf16[256,1536]{1,0:T(8,128)(2,1)S(1)}, u32[]{:S(2)}) copy-start(bf16[256,1536]{1,0:T(8,128)(2,1)S(1)} %collective-permute-done) | copy-start | bytes 2359300
  12.7 13.4 %collective-permute-start.1 = (bf16[256,1536]{1,0:T(8,128)(2,1)S(1)}, bf16[256,1536]{1,0:T(8,128)(2,1)S(1)}, u32[]{:S(2)}, u32[]{:S(2)}) collective-permute-start(bf16[256,1536]{1,0:T(8,128)(2,1)S(1)} %collective-permute-done), channel_id=1, source_target_pairs={{0,2},{2,4},{4,6},{6,8},{8,10},{10,12},{12,14},{14,16},{16,18},{18... | collective-permute-start | bytes 2359304 | tf_op jit(solution)/shard_map/ppermute | solution.py:16
  26.2 29.2 %copy-start.21 = (bf16[256,1536]{1,0:T(8,128)(2,1)}, bf16[256,1536]{1,0:T(8,128)(2,1)S(1)}, u32[]{:S(2)}) copy-start(bf16[256,1536]{1,0:T(8,128)(2,1)S(1)} %collective-permute-done.1) | copy-start | bytes 2359300
  26.2 18.8 %collective-permute-start.2 = (bf16[256,1536]{1,0:T(8,128)(2,1)S(1)}, bf16[256,1536]{1,0:T(8,128)(2,1)S(1)}, u32[]{:S(2)}, u32[]{:S(2)}) collective-permute-start(bf16[256,1536]{1,0:T(8,128)(2,1)S(1)} %collective-permute-done.1), channel_id=1, source_target_pairs={{0,2},{2,4},{4,6},{6,8},{8,10},{10,12},{12,14},{14,16},{16,18},{18... | collective-permute-start | bytes 2359304 | tf_op jit(solution)/shard_map/ppermute | solution.py:16
  44.0 138.1 %reduce-scatter.3.cloned.1.call-start = ((), (), s32[]{:S(2)}) async-start(), calls=%async_computation.3 | async-start | bytes 7077888 | tf_op jit(solution)/shard_map/reduce_scatter | solution.py:84
  45.0 10.5 %copy-start.19 = (bf16[256,1536]{1,0:T(8,128)(2,1)}, bf16[256,1536]{1,0:T(8,128)(2,1)S(1)}, u32[]{:S(2)}) copy-start(bf16[256,1536]{1,0:T(8,128)(2,1)S(1)} %collective-permute-done.2) | copy-start | bytes 2359300
  45.0 9.0 %collective-permute-start.3 = (bf16[256,1536]{1,0:T(8,128)(2,1)S(1)}, bf16[256,1536]{1,0:T(8,128)(2,1)}, u32[]{:S(2)}, u32[]{:S(2)}) collective-permute-start(bf16[256,1536]{1,0:T(8,128)(2,1)S(1)} %collective-permute-done.2), channel_id=1, source_target_pairs={{0,2},{2,4},{4,6},{6,8},{8,10},{10,12},{12,14},{14,16},{16,18},{18... | collective-permute-start | bytes 2359304 | tf_op jit(solution)/shard_map/ppermute | solution.py:16
  102.3 16.3 %copy-start.38 = (f32[256,12]{0,1:T(8,128)}, f32[256,12]{0,1:T(8,128)S(1)}, u32[]{:S(2)}) copy-start(f32[256,12]{0,1:T(8,128)S(1)} %get-tuple-element.39) | copy-start | bytes 36868
  106.0 166.3 %reduce-scatter.5.cloned.1.call-start = ((), (), s32[]{:S(2)}) async-start(), calls=%async_computation.4 | async-start | bytes 2506752 | tf_op jit(solution)/shard_map/reduce_scatter | solution.py:85
  109.5 9.1 %copy-start.37 = (pred[256,256]{0,1:T(8,128)(4,1)}, pred[256,256]{0,1:T(8,128)(4,1)S(1)}, u32[]{:S(2)}) copy-start(pred[256,256]{0,1:T(8,128)(4,1)S(1)} %get-tuple-element.32) | copy-start | bytes 196612
  125.3 6.1 %copy-start.20 = (bf16[256,1536]{1,0:T(8,128)(2,1)S(1)}, bf16[256,1536]{1,0:T(8,128)(2,1)}, u32[]{:S(2)}) copy-start(bf16[256,1536]{1,0:T(8,128)(2,1)} %copy-done.19) | copy-start | bytes 2359300
  130.1 15.3 %collective-permute-start.4 = (f32[256,1536]{1,0:T(8,128)}, f32[256,1536]{1,0:T(8,128)}, u32[]{:S(2)}, u32[]{:S(2)}) collective-permute-start(f32[256,1536]{1,0:T(8,128)} %pad_maximum_fusion), channel_id=1, source_target_pairs={{2,0},{4,2},{6,4},{8,6},{10,8},{12,10},{14,12},{16,14},{18,16},{20... | collective-permute-start | bytes 4718600 | tf_op jit(solution)/shard_map/ppermute | solution.py:16
  143.0 7.3 %copy-start.10 = (bf16[1,256,768]{1,2,0:T(8,128)(2,1)S(1)}, bf16[1,256,768]{1,2,0:T(8,128)(2,1)}, u32[]{:S(2)}) copy-start(bf16[1,256,768]{1,2,0:T(8,128)(2,1)} %copy.137) | copy-start | bytes 1179652
  148.7 24.9 %collective-permute-start.5 = (f32[256,1536]{1,0:T(8,128)}, f32[256,1536]{1,0:T(8,128)}, u32[]{:S(2)}, u32[]{:S(2)}) collective-permute-start(f32[256,1536]{1,0:T(8,128)} %maximum_add_fusion), channel_id=1, source_target_pairs={{2,0},{4,2},{6,4},{8,6},{10,8},{12,10},{14,12},{16,14},{18,16},{20... | collective-permute-start | bytes 4718600 | tf_op jit(solution)/shard_map/ppermute | solution.py:16
  173.6 5.7 %copy-start.36 = (pred[256,256]{0,1:T(8,128)(4,1)S(1)}, pred[256,256]{0,1:T(8,128)(4,1)}, u32[]{:S(2)}) copy-start(pred[256,256]{0,1:T(8,128)(4,1)} %get-tuple-element.34) | copy-start | bytes 196612
  176.6 16.2 %collective-permute-start.6 = (f32[256,1536]{1,0:T(8,128)}, f32[256,1536]{1,0:T(8,128)}, u32[]{:S(2)}, u32[]{:S(2)}) collective-permute-start(f32[256,1536]{1,0:T(8,128)} %maximum_add_fusion.1), channel_id=1, source_target_pairs={{2,0},{4,2},{6,4},{8,6},{10,8},{12,10},{14,12},{16,14},{18,16},{20... | collective-permute-start | bytes 4718600 | tf_op jit(solution)/shard_map/ppermute | solution.py:16
  182.1 6.1 %copy-start.40 = (f32[256,12]{0,1:T(8,128)S(1)}, f32[256,12]{0,1:T(8,128)}, u32[]{:S(2)}) copy-start(f32[256,12]{0,1:T(8,128)} %copy-done.38) | copy-start | bytes 36868
  195.5 22.1 %collective-permute-start.7 = (f32[256,1536]{1,0:T(8,128)}, f32[256,1536]{1,0:T(8,128)}, u32[]{:S(2)}, u32[]{:S(2)}) collective-permute-start(f32[256,1536]{1,0:T(8,128)} %maximum_add_fusion.2), channel_id=1, source_target_pairs={{2,0},{4,2},{6,4},{8,6},{10,8},{12,10},{14,12},{16,14},{18,16},{20... | collective-permute-start | bytes 4718600 | tf_op jit(solution)/shard_map/ppermute | solution.py:16
  207.7 10.0 %copy-start.29 = (f32[256,768]{1,0:T(8,128)S(1)}, f32[256,768]{1,0:T(8,128)}, u32[]{:S(2)}) copy-start(f32[256,768]{1,0:T(8,128)} %copy.160) | copy-start | bytes 2359300
  207.7 10.0 %copy-start.30 = (f32[256,768]{1,0:T(8,128)S(1)}, f32[256,768]{1,0:T(8,128)}, u32[]{:S(2)}) copy-start(f32[256,768]{1,0:T(8,128)} %copy.161) | copy-start | bytes 2359300
  208.6 63.7 %copy-start.1 = (bf16[1,256,1536]{2,1,0:T(8,128)(2,1)S(1)}, bf16[1,256,1536]{2,1,0:T(8,128)(2,1)}, u32[]{:S(2)}) copy-start(bf16[1,256,1536]{2,1,0:T(8,128)(2,1)} %param.9) | copy-start | bytes 2359300
  (28 other events, 79.8 us)
Sparse Core Ops, SparseCore 0:
  44.1 45.5 all-gather.1
  106.1 68.8 reduce-scatter.2
  182.3 90.0 reduce-scatter.4
where the time goes:
time: 280 us; the launch traced here: 279 us
  matrix products  74.8 us (27%)
  waiting for transfers between devices  70.7 us (25%)
  local copies, waits for them, and re-layouts  49.1 us (18%)
  starting transfers between devices  38.1 us (14%)
  other arithmetic  25.5 us (9%)
  between operations  14.4 us (5%)
  blocking collectives  6.32 us (2%)
    reduce_scatter x1, waiting for transfers between devices, local(): lax.psum_scatter(col_share, 'seq', scatter_dimension=0, tiled=True)  52.1 us
    ppermute x8, starting transfers between devices, shift_up(): return lax.ppermute(block, axis, route)  37.7 us
    dot_general x5, matrix products, local(): jnp.einsum('hqk,qhe->khe', prob_back, grad_heads, preferred_element_type=...  15.6 us
    reshape x5, local copies, waits for them, and re-layouts, local(): value_part.reshape(tok_rows, feature_width)  11.7 us
    ppermute x8, waiting for transfers between devices, shift_up(): return lax.ppermute(block, axis, route)  11 us
    dot_general x5, matrix products, local(): jnp.einsum('qhe,khe->hqk', grad_heads, value_block, preferred_element_typ...  10.1 us
    dot_general x1, matrix products, local(): jnp.einsum('hqk,khe->qhe', expo_full.astype(jnp.bfloat16), value_window,...  9.96 us
    dot_general x1, matrix products, local(): jnp.einsum('qhe,khe->hqk', query_heads, key_window, preferred_element_typ...  9.62 us
  transfers between devices with their start and end apart: 11, of which 6 were waited for; matrix products, arithmetic and copies ran while one was open for 46% of the time, Pallas kernels for 0%

commit v1 on v0

--- a/solution.py
+++ b/solution.py
@@ -8,6 +8,14 @@
 STRETCH = 128
 MOST = 1024
 MASKED_SCORE = -1e30
+
+
+def switch_tracks_all(array_in, join_dim):
+    array_in = jnp.moveaxis(array_in, 0, join_dim)
+    tmp = array_in.shape
+    return array_in.reshape(
+        *tmp[:join_dim], tmp[join_dim] * tmp[join_dim + 1], *tmp[join_dim + 2 :]
+    )
 
 
 def shift_up(block, axis, distance):
@@ -35,7 +43,19 @@
     score_scale = HEAD_DIM ** (-0.5)
     utt_lengths = lengths[0]
     weight_cols = lax.all_gather(out_weight, "dp", axis=1, tiled=True)
-    weight_full = lax.all_gather(weight_cols, "seq", axis=0, tiled=True)
+    num = lax.axis_size("seq")
+    chunks = tuple(((dev, (dev + 1) % num) for dev in range(num)))
+    xs_all = tuple(((rr, hop_no) for hop_no, rr in chunks))
+    val2, mat_out = ([], [])
+    for b in range(num - 1):
+        if b % 2 == 0:
+            val2.append(lax.ppermute(val2[-1] if val2 else weight_cols, "seq", chunks))
+        else:
+            mat_out.append(lax.ppermute(mat_out[-1] if mat_out else weight_cols, "seq", xs_all))
+    big = jnp.stack([*val2[::-1], weight_cols, *mat_out], 0)
+    next_value = lax.axis_index("seq") - len(val2)
+    big = big[(jnp.arange(num) - next_value) % num]
+    weight_full = switch_tracks_all(big, 0)
     query_heads = query_rows[0].reshape(tok_rows, HEADS, HEAD_DIM)
     key_value = jnp.concatenate([key_rows[0], value_rows[0]], axis=1)
     held = [key_value]

time: 280 us -> 318 us (1.14)
  local copies, waits for them, and re-layouts: 49.1 us -> 67.7 us
  waiting for transfers between devices: 70.7 us -> 85 us
  starting transfers between devices: 38.1 us -> 46.5 us
  matrix products: 74.8 us -> 70.8 us
    ppermute x0 -> x15, starting transfers between devices: none -> 32.3 us  [the longest x7 32.3 us: local(): lax.ppermute(mat_out[-1] if mat_out else weight_cols, 'seq', xs_all)]
    ppermute x8, starting transfers between devices: 37.7 us -> 13.9 us  [shift_up(): return lax.ppermute(block, axis, route)]
    unnamed x90 -> x131, local copies, waits for them, and re-layouts: 9.62 us -> 31.8 us
    ppermute x0 -> x15, waiting for transfers between devices: none -> 19 us  [the longest x8 14.7 us: local(): val2.append(lax.ppermute(val2[-1] if val2 else weight_cols, 'seq', chunks))]
    all_gather x1 -> x0, waiting for transfers between devices: 7.5 us -> none  [local(): weight_full = lax.all_gather(weight_cols, 'seq', axis=0, tiled=True)]
    ppermute x8, waiting for transfers between devices: 11 us -> 16.2 us  [shift_up(): return lax.ppermute(block, axis, route)]
    reshape x5, local copies, waits for them, and re-layouts: 11.7 us -> 6.65 us  [local(): value_part.reshape(tok_rows, feature_width)]
    dot_general x5, matrix products: 15.6 us -> 12 us  [local(): jnp.einsum('hqk,qhe->khe', prob_back, grad_heads, preferred_element_type=...]
  transfers between devices with their start and end apart: 11 -> 25, of which waited for: 6 -> 16; matrix products, arithmetic and copies ran while one was open for 46% -> 37% of each run, Pallas kernels for 0% -> 0%
where the time goes in v1:
time: 318 us; the launch traced here: 316 us
  waiting for transfers between devices  85 us (27%)
  matrix products  70.8 us (22%)
  local copies, waits for them, and re-layouts  67.7 us (21%)
  starting transfers between devices  46.5 us (15%)
  other arithmetic  25.1 us (8%)
  between operations  14.9 us (5%)
  blocking collectives  6.33 us (2%)
    reduce_scatter x1, waiting for transfers between devices, local(): lax.psum_scatter(col_share, 'seq', scatter_dimension=0, tiled=True)  49.8 us
    ppermute x7, starting transfers between devices, local(): lax.ppermute(mat_out[-1] if mat_out else weight_cols, 'seq', xs_all)  32.3 us
    unnamed x131, local copies, waits for them, and re-layouts  31.8 us
    ppermute x8, waiting for transfers between devices, shift_up(): return lax.ppermute(block, axis, route)  16.2 us
    ppermute x8, waiting for transfers between devices, local(): val2.append(lax.ppermute(val2[-1] if val2 else weight_cols, 'seq', chunks))  14.7 us
    ppermute x8, starting transfers between devices, shift_up(): return lax.ppermute(block, axis, route)  13.9 us
    dot_general x5, matrix products, local(): jnp.einsum('qhe,khe->hqk', grad_heads, value_block, preferred_element_typ...  13.5 us
    dot_general x5, matrix products, local(): jnp.einsum('hqk,qhe->khe', prob_back, grad_heads, preferred_element_type=...  12 us
  transfers between devices with their start and end apart: 25, of which 16 were waited for; matrix products, arithmetic and copies ran while one was open for 37% of the time, Pallas kernels for 0%

profile of v1, /device:TPU:0, one launch (start us, length us, event | category | flops | bytes accessed | tf_op | source)
XLA Modules:
  0.0 316.4 jit_solution(13960345634651462236)
XLA Ops:
  7.2 6.3 %all_gather.3 = bf16[48,1536]{1,0:T(8,128)(2,1)S(1)} all-gather(bf16[48,768]{1,0:T(8,128)(2,1)} %param.11), channel_id=1, replica_groups=mesh['seq'=16,'dp'=2] {'dp'}, dimensions={1}, use_global_device_ids=true | all-gather | bytes 221184 | tf_op jit(solution)/shard_map/all_gather | solution.py:45
  13.6 4.4 %collective-permute-start.12 = (bf16[48,1536]{1,0:T(8,128)(2,1)S(1)}, bf16[48,1536]{1,0:T(8,128)(2,1)S(1)}, u32[]{:S(2)}, u32[]{:S(2)}) collective-permute-start(bf16[48,1536]{1,0:T(8,128)(2,1)S(1)} %all_gather.3), channel_id=1, source_target_pairs={{2,0},{4,2},{6,4},{8,6},{10,8},{12,10},{14,12},{16,14},{18,16},{20... | collective-permute-start | bytes 442376 | tf_op jit(solution)/shard_map/ppermute | solution.py:54
  23.5 4.7 %collective-permute-done.5 = bf16[48,1536]{1,0:T(8,128)(2,1)S(1)} collective-permute-done((bf16[48,1536]{1,0:T(8,128)(2,1)S(1)}, bf16[48,1536]{1,0:T(8,128)(2,1)S(1)}, u32[]{:S(2)}, u32[]{:S(2)}) %collective-permute-start.5) | collective-permute-done | bytes 147488 | tf_op jit(solution)/shard_map/ppermute | solution.py:52
  29.2 4.4 %collective-permute-start.13 = (bf16[48,1536]{1,0:T(8,128)(2,1)S(1)}, bf16[48,1536]{1,0:T(8,128)(2,1)S(1)}, u32[]{:S(2)}, u32[]{:S(2)}) collective-permute-start(bf16[48,1536]{1,0:T(8,128)(2,1)S(1)} %collective-permute-done.12), channel_id=1, source_target_pairs={{2,0},{4,2},{6,4},{8,6},{10,8},{12,10},{14,12},{16,14},{18,16},{20... | collective-permute-start | bytes 442376 | tf_op jit(solution)/shard_map/ppermute | solution.py:54
  37.0 4.6 %collective-permute-start.14 = (bf16[48,1536]{1,0:T(8,128)(2,1)S(1)}, bf16[48,1536]{1,0:T(8,128)(2,1)S(1)}, u32[]{:S(2)}, u32[]{:S(2)}) collective-permute-start(bf16[48,1536]{1,0:T(8,128)(2,1)S(1)} %collective-permute-done.13), channel_id=1, source_target_pairs={{2,0},{4,2},{6,4},{8,6},{10,8},{12,10},{14,12},{16,14},{18,16},{20... | collective-permute-start | bytes 442376 | tf_op jit(solution)/shard_map/ppermute | solution.py:54
  44.9 4.7 %collective-permute-start.15 = (bf16[48,1536]{1,0:T(8,128)(2,1)S(1)}, bf16[48,1536]{1,0:T(8,128)(2,1)}, u32[]{:S(2)}, u32[]{:S(2)}) collective-permute-start(bf16[48,1536]{1,0:T(8,128)(2,1)S(1)} %collective-permute-done.14), channel_id=1, source_target_pairs={{2,0},{4,2},{6,4},{8,6},{10,8},{12,10},{14,12},{16,14},{18,16},{20... | collective-permute-start | bytes 442376 | tf_op jit(solution)/shard_map/ppermute | solution.py:54
  52.3 4.7 %collective-permute-start.16 = (bf16[48,1536]{1,0:T(8,128)(2,1)}, bf16[48,1536]{1,0:T(8,128)(2,1)}, u32[]{:S(2)}, u32[]{:S(2)}) collective-permute-start(bf16[48,1536]{1,0:T(8,128)(2,1)} %collective-permute-done.15), channel_id=1, source_target_pairs={{2,0},{4,2},{6,4},{8,6},{10,8},{12,10},{14,12},{16,14},{18,16},{20... | collective-permute-start | bytes 442376 | tf_op jit(solution)/shard_map/ppermute | solution.py:54
  60.0 4.7 %collective-permute-start.17 = (bf16[48,1536]{1,0:T(8,128)(2,1)}, bf16[48,1536]{1,0:T(8,128)(2,1)}, u32[]{:S(2)}, u32[]{:S(2)}) collective-permute-start(bf16[48,1536]{1,0:T(8,128)(2,1)} %collective-permute-done.16), channel_id=1, source_target_pairs={{2,0},{4,2},{6,4},{8,6},{10,8},{12,10},{14,12},{16,14},{18,16},{20... | collective-permute-start | bytes 442376 | tf_op jit(solution)/shard_map/ppermute | solution.py:54
  67.7 4.7 %collective-permute-start.18 = (bf16[48,1536]{1,0:T(8,128)(2,1)}, bf16[48,1536]{1,0:T(8,128)(2,1)S(1)}, u32[]{:S(2)}, u32[]{:S(2)}) collective-permute-start(bf16[48,1536]{1,0:T(8,128)(2,1)} %collective-permute-done.17), channel_id=1, source_target_pairs={{2,0},{4,2},{6,4},{8,6},{10,8},{12,10},{14,12},{16,14},{18,16},{20... | collective-permute-start | bytes 442376 | tf_op jit(solution)/shard_map/ppermute | solution.py:54
  93.9 3.2 %collective-permute-start.3 = (bf16[256,1536]{1,0:T(8,128)(2,1)}, bf16[256,1536]{1,0:T(8,128)(2,1)}, u32[]{:S(2)}, u32[]{:S(2)}) collective-permute-start(bf16[256,1536]{1,0:T(8,128)(2,1)} %collective-permute-done.2), channel_id=1, source_target_pairs={{0,2},{2,4},{4,6},{6,8},{8,10},{10,12},{12,14},{14,16},{16,18},{18... | collective-permute-start | bytes 2359304 | tf_op jit(solution)/shard_map/ppermute | solution.py:24
  107.8 4.0 %copy.115 = bf16[1280,768]{0,1:T(8,128)(2,1)} copy(bf16[1280,768]{1,0:T(8,128)(2,1)} %get-tuple-element.20) | data formatting | bytes 3932160 | tf_op jit(solution)/shard_map/slice | solution.py:65
  114.0 9.5 %fusion = (f32[12,256]{1,0:T(8,128)S(1)}, f32[12,1280,256]{2,1,0:T(8,128)}) fusion(pred[256,1280]{0,1:T(8,128)(4,1)S(1)} %copy-done.8, bf16[1280,12,64]{0,2,1:T(8,128)(2,1)} %bitcast.228, bf16[256,12,64]{0,2,1:T(8,128)(2,1)S(1)} %bitcast.215), kind=kOutput, calls=%fused_computation.3 | convolution fusion | flops 515109888 | bytes 18427904 | tf_op jit(solution)/shard_map/qhe,khe->hqk/dot_general | solution.py:75
  123.6 9.3 %fusion.1 = f32[12,256]{1,0:T(8,128)S(1)} fusion(f32[12,1280,256]{2,1,0:T(8,128)} %get-tuple-element.38, f32[12,256]{1,0:T(8,128)S(1)} %get-tuple-element.37, pred[256,1280]{0,1:T(8,128)(4,1)S(1)} %copy-done.8), kind=kLoop, calls=%fused_computation.4 | loop fusion | flops 19657728 | bytes 16080896 | tf_op jit(solution)/shard_map/reduce_sum | solution.py:81
  132.9 7.7 %multiply_reduce_fusion = (f32[256,12]{0,1:T(8,128)S(1)}, bf16[256,12,64]{0,2,1:T(8,128)(2,1)S(1)}) fusion(bf16[256,12,64]{0,2,1:T(8,128)(2,1)S(1)} %bitcast.255, f32[256,12]{0,1:T(8,128)S(1)} %bitcast.273, bf16[1280,12,64]{0,2,1:T(8,128)(2,1)S(1)} %bitcast.251, f32[12,1280,256]{2,1,0:T(8,128)} %get-tuple-element.38, f32[12,256]{1,0:T(8,128)S(1)} %get-tuple-element.37, ...), kind=kOutput, calls=%fused_computation.76 | convolution fusion | flops 524153856 | bytes 18845696 | tf_op jit(solution)/shard_map/hqk,khe->qhe/dot_general | solution.py:82
  159.7 3.0 multiply_convert_fusion.4
  175.0 3.1 multiply_convert_fusion.3
  189.1 3.7 %copy.135 = f32[12,256,256]{1,2,0:T(8,128)} copy(f32[12,256,256]{2,1,0:T(8,128)} %subtract_exponential_fusion) | data formatting | bytes 6291456 | tf_op jit(solution)/shard_map/exp | solution.py:123
  196.5 3.2 %multiply_convert_fusion.2 = bf16[12,256,256]{1,2,0:T(8,128)(2,1)S(1)} fusion(f32[12,256,256]{2,1,0:T(8,128)} %fusion.86, bf16[256,12,64]{0,2,1:T(8,128)(2,1)} %bitcast.252, bf16[256,12,64]{0,2,1:T(8,128)(2,1)} %bitcast.270, f32[12,256]{1,0:T(8,128)} %bitcast.276, f32[12,256]{1,0:T(8,128)S(1)} %log_add_fusion, pred[256,256]{0,1:T(8,128)(4,1)} %get-tuple-element.35), kind=kOutput, calls=%fused_computation.15 | convolution fusion | flops 105381888 | bytes 5595136 | tf_op jit(solution)/shard_map/qhe,khe->hqk/dot_general | solution.py:125
  203.6 3.6 %fusion.11 = f32[12,64,256]{2,1,0:T(8,128)} fusion(bf16[256,12,64]{0,2,1:T(8,128)(2,1)} %bitcast.253, f32[12,256,256]{2,1,0:T(8,128)} %fusion.88, f32[12,256]{1,0:T(8,128)S(1)} %log_add_fusion, pred[256,256]{0,1:T(8,128)(4,1)} %get-tuple-element.34), kind=kOutput, calls=%fused_computation.25 | convolution fusion | flops 103809024 | bytes 4403200 | tf_op jit(solution)/shard_map/hqk,qhe->khe/dot_general | solution.py:138
  209.5 3.3 %maximum_add_fusion.1 = f32[256,1536]{1,0:T(8,128)} fusion(f32[256,1536]{1,0:T(8,128)} %collective-permute-done.20, f32[256,768]{1,0:T(8,128)} %copy.150, f32[256,768]{1,0:T(8,128)} %copy.149), kind=kLoop, calls=%fused_computation.32 | loop fusion | flops 786432 | bytes 4718592 | tf_op jit(solution)/shard_map/add | solution.py:151
  227.2 4.9 %collective-permute-done.21 = f32[256,1536]{1,0:T(8,128)} collective-permute-done((f32[256,1536]{1,0:T(8,128)}, f32[256,1536]{1,0:T(8,128)}, u32[]{:S(2)}, u32[]{:S(2)}) %collective-permute-start.21) | collective-permute-done | bytes 1572896 | tf_op jit(solution)/shard_map/ppermute | solution.py:24
  242.3 3.5 %fusion.6 = bf16[1,256,1536]{2,1,0:T(8,128)(2,1)} fusion(bf16[256,768]{0,1:T(8,128)(2,1)} %bitcast.250, bf16[768,1536]{1,0:T(8,128)(2,1)} %bitcast.227), kind=kOutput, calls=%fused_computation.20 | convolution fusion | flops 604372992 | bytes 3538944 | tf_op jit(solution)/shard_map/dot_general | solution.py:94
  245.9 11.4 %collective-permute-done.22 = f32[256,1536]{1,0:T(8,128)} collective-permute-done((f32[256,1536]{1,0:T(8,128)}, f32[256,1536]{1,0:T(8,128)}, u32[]{:S(2)}, u32[]{:S(2)}) %collective-permute-start.22) | collective-permute-done | bytes 1572896 | tf_op jit(solution)/shard_map/ppermute | solution.py:24
  259.7 49.8 %reduce-scatter.5.cloned.1.call-done = f32[48,768]{1,0:T(8,128)} async-done(((f32[768,768]{1,0:T(8,128)}), f32[48,768]{1,0:T(8,128)}) %reduce-scatter.5.cloned.1.call-update) | async-done | bytes 147472 | tf_op jit(solution)/shard_map/reduce_scatter | solution.py:105
  (239 shorter events, 135.0 us)
Async XLA Ops:
  7.2 217.0 %reduce-scatter.3.cloned.1.call-start = ((), (), s32[]{:S(2)}) async-start(), calls=%async_computation.2 | async-start | bytes 7077888 | tf_op jit(solution)/shard_map/reduce_scatter | solution.py:104
  13.6 7.4 %collective-permute-start.4 = (bf16[48,1536]{1,0:T(8,128)(2,1)S(1)}, bf16[48,1536]{1,0:T(8,128)(2,1)S(1)}, u32[]{:S(2)}, u32[]{:S(2)}) collective-permute-start(bf16[48,1536]{1,0:T(8,128)(2,1)S(1)} %all_gather.3), channel_id=1, source_target_pairs={{0,2},{2,4},{4,6},{6,8},{8,10},{10,12},{12,14},{14,16},{16,18},{18... | collective-permute-start | bytes 442376 | tf_op jit(solution)/shard_map/ppermute | solution.py:52
  13.6 15.6 %collective-permute-start.12 = (bf16[48,1536]{1,0:T(8,128)(2,1)S(1)}, bf16[48,1536]{1,0:T(8,128)(2,1)S(1)}, u32[]{:S(2)}, u32[]{:S(2)}) collective-permute-start(bf16[48,1536]{1,0:T(8,128)(2,1)S(1)} %all_gather.3), channel_id=1, source_target_pairs={{2,0},{4,2},{6,4},{8,6},{10,8},{12,10},{14,12},{16,14},{18,16},{20... | collective-permute-start | bytes 442376 | tf_op jit(solution)/shard_map/ppermute | solution.py:54
  20.9 7.3 %collective-permute-start.5 = (bf16[48,1536]{1,0:T(8,128)(2,1)S(1)}, bf16[48,1536]{1,0:T(8,128)(2,1)S(1)}, u32[]{:S(2)}, u32[]{:S(2)}) collective-permute-start(bf16[48,1536]{1,0:T(8,128)(2,1)S(1)} %collective-permute-done.4), channel_id=1, source_target_pairs={{0,2},{2,4},{4,6},{6,8},{8,10},{10,12},{12,14},{14,16},{16,18},{18... | collective-permute-start | bytes 442376 | tf_op jit(solution)/shard_map/ppermute | solution.py:52
  22.2 43.7 %collective-permute-start = (bf16[256,1536]{1,0:T(8,128)(2,1)S(1)}, bf16[256,1536]{1,0:T(8,128)(2,1)S(1)}, u32[]{:S(2)}, u32[]{:S(2)}) collective-permute-start(bf16[256,1536]{1,0:T(8,128)(2,1)S(1)} %pad_maximum_fusion.1), channel_id=1, source_target_pairs={{0,2},{2,4},{4,6},{6,8},{8,10},{10,12},{12,14},{14,16},{16,18},{18... | collective-permute-start | bytes 2359304 | tf_op jit(solution)/shard_map/ppermute | solution.py:24
  28.2 7.4 %collective-permute-start.6 = (bf16[48,1536]{1,0:T(8,128)(2,1)S(1)}, bf16[48,1536]{1,0:T(8,128)(2,1)}, u32[]{:S(2)}, u32[]{:S(2)}) collective-permute-start(bf16[48,1536]{1,0:T(8,128)(2,1)S(1)} %collective-permute-done.5), channel_id=1, source_target_pairs={{0,2},{2,4},{4,6},{6,8},{8,10},{10,12},{12,14},{14,16},{16,18},{18... | collective-permute-start | bytes 442376 | tf_op jit(solution)/shard_map/ppermute | solution.py:52
  29.2 7.1 %collective-permute-start.13 = (bf16[48,1536]{1,0:T(8,128)(2,1)S(1)}, bf16[48,1536]{1,0:T(8,128)(2,1)S(1)}, u32[]{:S(2)}, u32[]{:S(2)}) collective-permute-start(bf16[48,1536]{1,0:T(8,128)(2,1)S(1)} %collective-permute-done.12), channel_id=1, source_target_pairs={{2,0},{4,2},{6,4},{8,6},{10,8},{12,10},{14,12},{16,14},{18,16},{20... | collective-permute-start | bytes 442376 | tf_op jit(solution)/shard_map/ppermute | solution.py:54
  35.6 7.6 %collective-permute-start.7 = (bf16[48,1536]{1,0:T(8,128)(2,1)}, bf16[48,1536]{1,0:T(8,128)(2,1)S(1)}, u32[]{:S(2)}, u32[]{:S(2)}) collective-permute-start(bf16[48,1536]{1,0:T(8,128)(2,1)} %collective-permute-done.6), channel_id=1, source_target_pairs={{0,2},{2,4},{4,6},{6,8},{8,10},{10,12},{12,14},{14,16},{16,18},{18... | collective-permute-start | bytes 442376 | tf_op jit(solution)/shard_map/ppermute | solution.py:52
  37.0 7.3 %collective-permute-start.14 = (bf16[48,1536]{1,0:T(8,128)(2,1)S(1)}, bf16[48,1536]{1,0:T(8,128)(2,1)S(1)}, u32[]{:S(2)}, u32[]{:S(2)}) collective-permute-start(bf16[48,1536]{1,0:T(8,128)(2,1)S(1)} %collective-permute-done.13), channel_id=1, source_target_pairs={{2,0},{4,2},{6,4},{8,6},{10,8},{12,10},{14,12},{16,14},{18,16},{20... | collective-permute-start | bytes 442376 | tf_op jit(solution)/shard_map/ppermute | solution.py:54
  43.2 7.4 %collective-permute-start.8 = (bf16[48,1536]{1,0:T(8,128)(2,1)S(1)}, bf16[48,1536]{1,0:T(8,128)(2,1)S(1)}, u32[]{:S(2)}, u32[]{:S(2)}) collective-permute-start(bf16[48,1536]{1,0:T(8,128)(2,1)S(1)} %collective-permute-done.7), channel_id=1, source_target_pairs={{0,2},{2,4},{4,6},{6,8},{8,10},{10,12},{12,14},{14,16},{16,18},{18... | collective-permute-start | bytes 442376 | tf_op jit(solution)/shard_map/ppermute | solution.py:52
  44.9 7.4 %collective-permute-start.15 = (bf16[48,1536]{1,0:T(8,128)(2,1)S(1)}, bf16[48,1536]{1,0:T(8,128)(2,1)}, u32[]{:S(2)}, u32[]{:S(2)}) collective-permute-start(bf16[48,1536]{1,0:T(8,128)(2,1)S(1)} %collective-permute-done.14), channel_id=1, source_target_pairs={{2,0},{4,2},{6,4},{8,6},{10,8},{12,10},{14,12},{16,14},{18,16},{20... | collective-permute-start | bytes 442376 | tf_op jit(solution)/shard_map/ppermute | solution.py:54
  50.5 7.5 %collective-permute-start.9 = (bf16[48,1536]{1,0:T(8,128)(2,1)S(1)}, bf16[48,1536]{1,0:T(8,128)(2,1)}, u32[]{:S(2)}, u32[]{:S(2)}) collective-permute-start(bf16[48,1536]{1,0:T(8,128)(2,1)S(1)} %collective-permute-done.8), channel_id=1, source_target_pairs={{0,2},{2,4},{4,6},{6,8},{8,10},{10,12},{12,14},{14,16},{16,18},{18... | collective-permute-start | bytes 442376 | tf_op jit(solution)/shard_map/ppermute | solution.py:52
  52.3 7.7 %collective-permute-start.16 = (bf16[48,1536]{1,0:T(8,128)(2,1)}, bf16[48,1536]{1,0:T(8,128)(2,1)}, u32[]{:S(2)}, u32[]{:S(2)}) collective-permute-start(bf16[48,1536]{1,0:T(8,128)(2,1)} %collective-permute-done.15), channel_id=1, source_target_pairs={{2,0},{4,2},{6,4},{8,6},{10,8},{12,10},{14,12},{16,14},{18,16},{20... | collective-permute-start | bytes 442376 | tf_op jit(solution)/shard_map/ppermute | solution.py:54
  58.0 7.6 %collective-permute-start.10 = (bf16[48,1536]{1,0:T(8,128)(2,1)}, bf16[48,1536]{1,0:T(8,128)(2,1)}, u32[]{:S(2)}, u32[]{:S(2)}) collective-permute-start(bf16[48,1536]{1,0:T(8,128)(2,1)} %collective-permute-done.9), channel_id=1, source_target_pairs={{0,2},{2,4},{4,6},{6,8},{8,10},{10,12},{12,14},{14,16},{16,18},{18... | collective-permute-start | bytes 442376 | tf_op jit(solution)/shard_map/ppermute | solution.py:52
  60.0 7.7 %collective-permute-start.17 = (bf16[48,1536]{1,0:T(8,128)(2,1)}, bf16[48,1536]{1,0:T(8,128)(2,1)}, u32[]{:S(2)}, u32[]{:S(2)}) collective-permute-start(bf16[48,1536]{1,0:T(8,128)(2,1)} %collective-permute-done.16), channel_id=1, source_target_pairs={{2,0},{4,2},{6,4},{8,6},{10,8},{12,10},{14,12},{16,14},{18,16},{20... | collective-permute-start | bytes 442376 | tf_op jit(solution)/shard_map/ppermute | solution.py:54
  65.6 7.6 %collective-permute-start.11 = (bf16[48,1536]{1,0:T(8,128)(2,1)}, bf16[48,1536]{1,0:T(8,128)(2,1)}, u32[]{:S(2)}, u32[]{:S(2)}) collective-permute-start(bf16[48,1536]{1,0:T(8,128)(2,1)} %collective-permute-done.10), channel_id=1, source_target_pairs={{0,2},{2,4},{4,6},{6,8},{8,10},{10,12},{12,14},{14,16},{16,18},{18... | collective-permute-start | bytes 442376 | tf_op jit(solution)/shard_map/ppermute | solution.py:52
  65.9 22.6 %collective-permute-start.1 = (bf16[256,1536]{1,0:T(8,128)(2,1)S(1)}, bf16[256,1536]{1,0:T(8,128)(2,1)S(1)}, u32[]{:S(2)}, u32[]{:S(2)}) collective-permute-start(bf16[256,1536]{1,0:T(8,128)(2,1)S(1)} %collective-permute-done), channel_id=1, source_target_pairs={{0,2},{2,4},{4,6},{6,8},{8,10},{10,12},{12,14},{14,16},{16,18},{18... | collective-permute-start | bytes 2359304 | tf_op jit(solution)/shard_map/ppermute | solution.py:24
  67.7 31.0 %collective-permute-start.18 = (bf16[48,1536]{1,0:T(8,128)(2,1)}, bf16[48,1536]{1,0:T(8,128)(2,1)S(1)}, u32[]{:S(2)}, u32[]{:S(2)}) collective-permute-start(bf16[48,1536]{1,0:T(8,128)(2,1)} %collective-permute-done.17), channel_id=1, source_target_pairs={{2,0},{4,2},{6,4},{8,6},{10,8},{12,10},{14,12},{16,14},{18,16},{20... | collective-permute-start | bytes 442376 | tf_op jit(solution)/shard_map/ppermute | solution.py:54
  93.9 9.4 %collective-permute-start.3 = (bf16[256,1536]{1,0:T(8,128)(2,1)}, bf16[256,1536]{1,0:T(8,128)(2,1)}, u32[]{:S(2)}, u32[]{:S(2)}) collective-permute-start(bf16[256,1536]{1,0:T(8,128)(2,1)} %collective-permute-done.2), channel_id=1, source_target_pairs={{0,2},{2,4},{4,6},{6,8},{8,10},{10,12},{12,14},{14,16},{16,18},{18... | collective-permute-start | bytes 2359304 | tf_op jit(solution)/shard_map/ppermute | solution.py:24
  144.3 165.2 %reduce-scatter.5.cloned.1.call-start = ((), (), s32[]{:S(2)}) async-start(), calls=%async_computation.3 | async-start | bytes 2506752 | tf_op jit(solution)/shard_map/reduce_scatter | solution.py:105
  168.2 14.1 %collective-permute-start.19 = (f32[256,1536]{1,0:T(8,128)}, f32[256,1536]{1,0:T(8,128)}, u32[]{:S(2)}, u32[]{:S(2)}) collective-permute-start(f32[256,1536]{1,0:T(8,128)} %pad_maximum_fusion), channel_id=1, source_target_pairs={{2,0},{4,2},{6,4},{8,6},{10,8},{12,10},{14,12},{16,14},{18,16},{20... | collective-permute-start | bytes 4718600 | tf_op jit(solution)/shard_map/ppermute | solution.py:24
  185.1 24.4 %collective-permute-start.20 = (f32[256,1536]{1,0:T(8,128)}, f32[256,1536]{1,0:T(8,128)}, u32[]{:S(2)}, u32[]{:S(2)}) collective-permute-start(f32[256,1536]{1,0:T(8,128)} %maximum_add_fusion), channel_id=1, source_target_pairs={{2,0},{4,2},{6,4},{8,6},{10,8},{12,10},{14,12},{16,14},{18,16},{20... | collective-permute-start | bytes 4718600 | tf_op jit(solution)/shard_map/ppermute | solution.py:24
  212.8 19.2 %collective-permute-start.21 = (f32[256,1536]{1,0:T(8,128)}, f32[256,1536]{1,0:T(8,128)}, u32[]{:S(2)}, u32[]{:S(2)}) collective-permute-start(f32[256,1536]{1,0:T(8,128)} %maximum_add_fusion.1), channel_id=1, source_target_pairs={{2,0},{4,2},{6,4},{8,6},{10,8},{12,10},{14,12},{16,14},{18,16},{20... | collective-permute-start | bytes 4718600 | tf_op jit(solution)/shard_map/ppermute | solution.py:24
  234.9 22.4 %collective-permute-start.22 = (f32[256,1536]{1,0:T(8,128)}, f32[256,1536]{1,0:T(8,128)}, u32[]{:S(2)}, u32[]{:S(2)}) collective-permute-start(f32[256,1536]{1,0:T(8,128)} %maximum_add_fusion.2), channel_id=1, source_target_pairs={{2,0},{4,2},{6,4},{8,6},{10,8},{12,10},{14,12},{16,14},{18,16},{20... | collective-permute-start | bytes 4718600 | tf_op jit(solution)/shard_map/ppermute | solution.py:24
  (55 other events, 551.7 us)
Sparse Core Ops, SparseCore 0:
  144.4 68.8 reduce-scatter.2
  224.3 85.1 reduce-scatter.4
